TPU v7x, 32 devices: a whole 2x2x4 slice. The times are simulated.
32 devices in a mesh: req: 8 (over y, x, core), tp: 4 (over z).
Axes of the slice: x: 2, y: 2, z: 4, core: 2. Of those that a mesh axis runs over, the one named last changes fastest.
Arguments:
- queries: bfloat16 [1536, 2560], P('req', 'tp'), may hold values from -5 to 5
- new_keys: bfloat16 [1536, 512], P('req', 'tp'), may hold values from -5 to 5
- new_values: bfloat16 [1536, 512], P('req', 'tp'), may hold values from -5 to 5
- key_pages: bfloat16 [512, 64, 512], P('req', None, 'tp'), may hold values from -5 to 5
- value_pages: bfloat16 [512, 64, 512], P('req', None, 'tp'), may hold values from -5 to 5
- page_table: int32 [32, 16], P('req'), may hold values from 0 to 511, as said below
- cache_lengths: int32 [32], P('req'), may hold values from 2 to 1024, as said below
- parents: int32 [32, 48], P('req'), may hold values from -1 to 46, as said below
- residual: bfloat16 [1536, 2560], P('req'), may hold values from -6 to 6
- out_weight: bfloat16 [2560, 2560], P('tp'), may hold values from -0.125 to 0.125
- norm_gain: float32 [2560], replicated, may hold values from 0.1 to 1.9
- router_weight: float32 [2560, 16], replicated, may hold values from -0.125 to 0.125
- routes: int32 [1536, 6], P('req'), may hold values from 0 to 15, all different within a row; in each aligned block of 192 rows (0 to 191, 192 to 383, ...) at most 91 rows name the same one
- expert_gate_up: bfloat16 [16, 2560, 2, 1536], P('req', None, None, 'tp'), may hold values from -0.125 to 0.125
- expert_down: bfloat16 [16, 1536, 2560], P('req', 'tp'), may hold values from -0.15625 to 0.15625
- shared_gate_up: bfloat16 [2560, 2, 1536], P(None, None, 'tp'), may hold values from -0.125 to 0.125
- shared_down: bfloat16 [1536, 2560], P('tp'), may hold values from -0.15625 to 0.15625
Outputs:
- layer_out: bfloat16 [1536, 2560], P('req', 'tp')
Inputs may be any that keep to these rules, and one draw needn't show every extreme that they name: `page_table`: the pages of the 4 requests of the d-th block of 4 rows are the d-th block of 64 pages of the pool, each named once. `cache_lengths`: some request holds 1024 positions. parents[r, 0] = -1, and 0 <= parents[r, i] < i for i >= 1. `routes`: A token's 6 experts differ. In each aligned block of 192 rows no expert is named by more than 91 rows, and in some block one expert is named by exactly 91.
All inputs are finite; a program needn't handle non-finite values.
Results may differ from a plain program's by a relative error of at most 0.02.
Values may be sent and summed in bfloat16 or wider, within the bound.
No kernel may reach another device: no remote copies, remote signals or barrier semaphores. Data moves between devices by JAX's collectives and lax.ppermute only.
A program may use at most 128 MiB of HBM per device.

v0:
```python
import math
import jax
import jax.numpy as jnp
from jax import lax
from jax.sharding import PartitionSpec as P

QH = 20
KVH = 4
HD = 128
EPSILON = 1e-06
NEGATIVE = -1e30


def rounded(values):
    return lax.optimization_barrier(values.astype(jnp.bfloat16)).astype(jnp.float32)


def ancestors(parents):
    tree_size = parents.shape[-1]
    position = jnp.arange(tree_size, dtype=jnp.int32)
    adjacency = (parents[..., :, None] == position[None, :]) | (
        position[:, None] == position[None, :]
    )
    closure = adjacency.astype(jnp.float32)
    for doubling in range(max(1, (tree_size - 1).bit_length())):
        closure = jnp.minimum(
            jnp.einsum("...ij,...jk->...ik", closure, closure, precision=lax.Precision.HIGHEST), 1.0
        )
    return closure > 0.5


def tree_attention(queries, cache_keys, cache_values, new_keys, new_values, lengths, allowed):
    scaling = 1.0 / math.sqrt(queries.shape[-1])
    cache_scores = (
        jnp.einsum("rtkgd,rckd->rkgtc", queries, cache_keys, preferred_element_type=jnp.float32)
        * scaling
    )
    tree_scores = (
        jnp.einsum("rtkgd,rskd->rkgts", queries, new_keys, preferred_element_type=jnp.float32)
        * scaling
    )
    live = jnp.arange(cache_keys.shape[1], dtype=jnp.int32)[None, :] < lengths[:, None]
    cache_scores = jnp.where(live[:, None, None, None, :], cache_scores, NEGATIVE)
    tree_scores = jnp.where(allowed[:, None, None, :, :], tree_scores, NEGATIVE)
    highest = jnp.maximum(jnp.max(cache_scores, axis=-1), jnp.max(tree_scores, axis=-1))[..., None]
    cache_exp = jnp.exp(cache_scores - highest)
    tree_exp = jnp.exp(tree_scores - highest)
    denominator = (jnp.sum(cache_exp, axis=-1) + jnp.sum(tree_exp, axis=-1))[..., None]
    cache_probs = (cache_exp / denominator).astype(jnp.bfloat16)
    tree_probs = (tree_exp / denominator).astype(jnp.bfloat16)
    mixed = jnp.einsum(
        "rkgtc,rckd->rtkgd", cache_probs, cache_values, preferred_element_type=jnp.float32
    )
    mixed = mixed + jnp.einsum(
        "rkgts,rskd->rtkgd", tree_probs, new_values, preferred_element_type=jnp.float32
    )
    return mixed.astype(jnp.bfloat16).reshape(queries.shape[0], queries.shape[1], -1)


def place_rows(routes, experts_local, groups, capacity):
    flat_expert = routes.reshape(-1)
    expert_ids = jnp.arange(experts_local * groups, dtype=jnp.int32)
    onehot = (flat_expert[:, None] == expert_ids[None, :]).astype(jnp.int32)
    earlier = jnp.cumsum(onehot, axis=0) - onehot
    rank = jnp.sum(earlier * onehot, axis=1)
    owner = flat_expert // experts_local
    local_expert = flat_expert % experts_local
    return (local_expert * groups + owner) * capacity + rank


def fill_outbox(row_values, slot_index, top_count, lead_shape):
    repeated = jnp.repeat(row_values, top_count, axis=0)
    outbox = jnp.zeros(
        (lead_shape[0] * lead_shape[1] * lead_shape[2], row_values.shape[1]), row_values.dtype
    )
    outbox = outbox.at[slot_index].set(repeated)
    return outbox.reshape(lead_shape + (row_values.shape[1],))


def shards(
    queries,
    new_keys,
    new_values,
    key_pages,
    value_pages,
    page_table,
    cache_lengths,
    parents,
    residual,
    out_weight,
    norm_gain,
    router_weight,
    routes,
    expert_gate_up,
    expert_down,
    shared_gate_up,
    shared_down,
):
    groups = lax.axis_size("req")
    tp_count = lax.axis_size("tp")
    requests = parents.shape[0]
    tree_size = parents.shape[1]
    row_count = requests * tree_size
    kv_local = new_keys.shape[1] // HD
    head_ratio = QH // KVH
    model_width = residual.shape[1]
    part_width = model_width // tp_count
    pages_dev = key_pages.shape[0]
    local_pages = page_table - lax.axis_index("req") * pages_dev
    cache_keys = key_pages[local_pages].reshape(requests, -1, kv_local, HD)
    cache_values = value_pages[local_pages].reshape(requests, -1, kv_local, HD)
    head_outputs = tree_attention(
        queries.reshape(requests, tree_size, kv_local, head_ratio, HD),
        cache_keys,
        cache_values,
        new_keys.reshape(requests, tree_size, kv_local, HD),
        new_values.reshape(requests, tree_size, kv_local, HD),
        cache_lengths,
        ancestors(parents),
    )
    attn_terms = jnp.dot(
        head_outputs.reshape(row_count, -1), out_weight, preferred_element_type=jnp.float32
    )
    column = lax.axis_index("tp") * part_width
    experts_local = expert_gate_up.shape[0]
    top_count = routes.shape[1]
    expert_count = experts_local * groups
    capacity = max(10 * requests, row_count * top_count * 5 // (4 * expert_count) + 1)
    slot_index = place_rows(routes, experts_local, groups, capacity)
    lead_shape = (experts_local, groups, capacity)
    attn_out = lax.psum(attn_terms.astype(jnp.bfloat16), "tp").astype(jnp.float32)
    hidden = rounded(residual.astype(jnp.float32) + attn_out)
    rstd = lax.rsqrt(jnp.mean(hidden * hidden, axis=1, keepdims=True) + EPSILON)
    normed = hidden * rstd * norm_gain
    logits = jnp.dot(normed, router_weight, precision=lax.Precision.HIGHEST)
    normed_bf = normed.astype(jnp.bfloat16)
    hidden_part = lax.dynamic_slice_in_dim(hidden, column, part_width, 1)
    outbox = fill_outbox(normed_bf, slot_index, top_count, lead_shape)
    arrived = lax.all_to_all(outbox, "req", split_axis=1, concat_axis=1, tiled=True)
    arrived = arrived.reshape(experts_local, groups * capacity, model_width)
    gate_up = jnp.einsum(
        "emd,edcf->emcf", arrived, expert_gate_up, preferred_element_type=jnp.float32
    )
    act = (jax.nn.silu(gate_up[:, :, 0]) * gate_up[:, :, 1]).astype(jnp.bfloat16)
    partial_value = rounded(
        jnp.einsum("emf,efd->emd", act, expert_down, preferred_element_type=jnp.float32)
    )
    summed = lax.psum_scatter(
        partial_value.astype(jnp.bfloat16), "tp", scatter_dimension=2, tiled=True
    )
    outputs = summed.reshape(experts_local, groups, capacity, part_width)
    returned = lax.all_to_all(outputs, "req", split_axis=1, concat_axis=1, tiled=True).reshape(
        -1, part_width
    )
    picked = returned[slot_index].astype(jnp.float32).reshape(row_count, top_count, part_width)
    expert_ids = jnp.arange(expert_count, dtype=jnp.int32)
    chosen = jnp.sum(
        jnp.where(routes[:, :, None] == expert_ids[None, None, :], logits[:, None, :], 0.0), axis=-1
    )
    gate_values = jax.nn.sigmoid(chosen)
    gate_values = gate_values / jnp.sum(gate_values, axis=1, keepdims=True)
    routed = jnp.sum(picked * gate_values[:, :, None], axis=1)
    shared_gu = jnp.einsum(
        "td,dcf->tcf", normed_bf, shared_gate_up, preferred_element_type=jnp.float32
    )
    shared_act = (jax.nn.silu(shared_gu[:, 0]) * shared_gu[:, 1]).astype(jnp.bfloat16)
    shared_terms = jnp.dot(shared_act, shared_down, preferred_element_type=jnp.float32)
    shared_out = lax.psum_scatter(
        shared_terms.astype(jnp.bfloat16), "tp", scatter_dimension=1, tiled=True
    ).astype(jnp.float32)
    return (hidden_part + shared_out + routed).astype(jnp.bfloat16)


def solution(mesh):
    in_specs = (
        P("req", "tp"),
        P("req", "tp"),
        P("req", "tp"),
        P("req", None, "tp"),
        P("req", None, "tp"),
        P("req", None),
        P("req"),
        P("req", None),
        P("req", None),
        P("tp", None),
        P(),
        P(),
        P("req", None),
        P("req", None, None, "tp"),
        P("req", "tp", None),
        P(None, None, "tp"),
        P("tp", None),
    )
    out_specs = P("req", "tp")
    return jax.shard_map(shards, mesh=mesh, in_specs=in_specs, out_specs=out_specs, check_vma=False)
```

profile of v0, /device:TPU:0, one launch (start us, length us, event | category | flops | bytes accessed | tf_op | source)
XLA Modules:
  0.0 486.2 jit_solution(5703992235077245131)
XLA Ops:
  6.6 0.8 compare_select_fusion.4
  7.5 0.8 iota_compare_fusion.5
  8.3 2.0 reshape.306
  10.2 1.0 convolution_minimum_fusion.5
  11.2 0.2 convolution_minimum_fusion.4
  11.5 0.2 convolution_minimum_fusion.3
  11.7 0.2 convolution_minimum_fusion.2
  11.9 0.2 convolution_minimum_fusion.1
  12.2 0.2 fusion.22
  12.4 0.1 copy.58
  12.5 2.9 gather_fusion.1
  15.4 2.1 bitcast_reduce_fusion
  17.6 0.4 fusion.55
  18.0 1.4 copy-done.2
  19.4 1.0 fusion.8
  20.4 0.1 fusion.28
  20.5 2.9 gather_fusion
  23.4 3.5 fusion.11
  26.9 0.3 fusion.21
  27.2 0.1 copy.61
  27.4 1.9 convolution_convert_fusion.2
  29.3 0.2 reduce-scatter.9.cloned.1.call-start
  29.6 0.1 copy.63
  29.7 0.1 eq.80
  29.8 0.1 eq.76
  30.0 0.1 reshape.311
  30.1 4.5 reduce-window.6
  34.7 0.4 slice_reduce_fusion
  35.1 0.2 reduce-window.9
  35.3 0.1 broadcast_add_fusion
  35.5 46.5 %all-reduce.2.cloned.1.call-done = bf16[192,2560]{1,0:T(8,128)(2,1)} async-done(((bf16[192,2560]{1,0:T(8,128)(2,1)}), bf16[192,2560]{1,0:T(8,128)(2,1)}) %all-reduce.2.cloned.1.call-update) | async-done | bytes 983056 | tf_op jit(solution)/shard_map/psum | solution.py:131
  82.0 1.7 add_convert_fusion
  83.7 0.3 multiply_reduce_fusion.1
  84.0 0.3 fusion.15
  84.3 4.0 broadcast_in_dim.72
  88.3 10.2 %reshape.347 = bf16[1152,2560]{1,0:T(8,128)(2,1)} reshape(bf16[192,6,2560]{2,1,0:T(8,128)(2,1)} %broadcast_in_dim.72) | data formatting | bytes 11796480 | tf_op jit(solution)/shard_map/reshape | solution.py:72
  98.5 17.2 %scatter_custom_fusion = bf16[1456,2560]{1,0:T(8,128)(2,1)} fusion(s32[1152]{0:T(1024)S(1)} %fusion.48, bf16[1152,2560]{1,0:T(8,128)(2,1)} %reshape.347, bf16[]{:T(256)} %constant.73.clone.1), kind=kCustom, calls=%fused_computation.18 | custom fusion | bytes 7455232 | tf_op jit(solution)/shard_map/scatter | solution.py:76
  115.7 6.3 %reshape.314 = bf16[2,8,91,2560]{3,2,1,0:T(8,128)(2,1)} reshape(bf16[1456,2560]{1,0:T(8,128)(2,1)} %scatter_custom_fusion) | data formatting | bytes 14909440 | tf_op jit(solution)/shard_map/reshape | solution.py:77
  121.9 27.5 %copy.66 = bf16[2,8,91,2560]{3,0,2,1:T(2,128)(2,1)S(1)} copy(bf16[2,8,91,2560]{3,2,1,0:T(8,128)(2,1)} %reshape.314) | data formatting | bytes 14909440 | tf_op jit(solution)/shard_map/reshape | solution.py:77
  149.4 87.5 %all_to_all.10 = bf16[2,8,91,2560]{3,0,2,1:T(2,128)(2,1)S(1)} all-to-all(bf16[2,8,91,2560]{3,0,2,1:T(2,128)(2,1)S(1)} %copy.66), channel_id=1, replica_groups=mesh['req'=8,'tp'=4] {'req'}, dimensions={1} | all-to-all | bytes 14909440 | tf_op jit(solution)/shard_map/all_to_all | solution.py:139
  236.9 9.0 %fusion = f32[2,728,2,384]{3,1,2,0:T(8,128)S(1)} fusion(bf16[2,2560,2,384]{3,2,1,0:T(2,128)(2,1)} %param.30, bf16[2,728,2560,1]{2,0,1,3:T(2,128)(2,1)S(1)} %bitcast.150), kind=kOutput, calls=%fused_computation.4 | convolution fusion | flops 5725224960 | bytes 19791872 | tf_op jit(solution)/shard_map/emd,edcf->emcf/dot_general | solution.py:141
  245.9 6.1 %convolution_convert_fusion = bf16[2,728,2560]{2,1,0:T(8,128)(2,1)} fusion(bf16[2,384,2560]{2,1,0:T(8,128)(2,1)S(1)} %copy-done.9, f32[2,728,2,384]{3,1,2,0:T(8,128)S(1)} %fusion), kind=kOutput, calls=%fused_computation.7 | convolution fusion | flops 2869694464 | bytes 15859712 | tf_op jit(solution)/shard_map/emf,efd->emd/dot_general | solution.py:146
  252.0 20.1 %copy.85 = bf16[2,728,2560]{1,0,2:T(2,128)(2,1)} copy(bf16[2,728,2560]{2,1,0:T(8,128)(2,1)} %convolution_convert_fusion) | data formatting | bytes 14909440
  272.1 18.3 %reshape.365 = bf16[2560,1456]{1,0:T(8,128)(2,1)} reshape(bf16[2560,2,728]{2,1,0:T(2,128)(2,1)} %bitcast.148) | data formatting | bytes 14909440
  290.5 0.3 reduce-scatter.7.cloned.1.call-start
  290.8 3.2 fusion.4
  294.0 0.7 convolution_convert_fusion.1
  294.7 1.4 copy.83
  296.1 128.2 %reduce-scatter.9.cloned.1.call-done = bf16[640,1456]{1,0:T(8,128)(2,1)} async-done(((bf16[2560,1456]{1,0:T(8,128)(2,1)}), bf16[640,1456]{1,0:T(8,128)(2,1)}) %reduce-scatter.9.cloned.1.call-update) | async-done | bytes 1863696
  424.4 5.2 %reshape.366 = bf16[640,2,728]{2,1,0:T(2,128)(2,1)S(1)} reshape(bf16[640,1456]{1,0:T(8,128)(2,1)} %reduce-scatter.9.cloned.1.call-done) | data formatting | bytes 3727360
  429.5 5.0 %copy.82 = bf16[2,728,640]{2,0,1:T(2,128)(2,1)} copy(bf16[2,728,640]{1,0,2:T(2,128)(2,1)S(1)} %bitcast.149) | data formatting | bytes 3727360 | tf_op jit(solution)/shard_map/reshape | solution.py:151
  434.5 3.8 all-to-all-start.1
  438.3 1.5 convert_element_type.77
  439.8 1.8 fusion.14
  441.7 0.8 copy.72
  442.4 16.1 %reduce-scatter.7.cloned.1.call-done = bf16[640,192]{1,0:T(8,128)(2,1)} async-done(((bf16[2560,192]{1,0:T(8,128)(2,1)}), bf16[640,192]{1,0:T(8,128)(2,1)}) %reduce-scatter.7.cloned.1.call-update) | async-done | bytes 245776
  458.5 1.1 copy.84
  459.7 2.7 all-to-all-done.1
  462.4 1.5 copy.71
  463.9 1.8 reshape.317
  465.8 4.8 gather_fusion.2
  470.6 4.0 reshape.318
  474.5 3.4 multiply_reduce_fusion
  477.9 1.8 add_convert_fusion.1
  (42 shorter events, 0.4 us)
Async XLA Ops:
  6.5 20.8 %copy-start = (bf16[640,2560]{1,0:T(8,128)(2,1)S(1)}, bf16[640,2560]{1,0:T(8,128)(2,1)}, u32[]{:S(2)}) copy-start(bf16[640,2560]{1,0:T(8,128)(2,1)} %param.26) | copy-start | bytes 9830404
  6.5 75.4 %all-reduce.2.cloned.1.call-start = ((), (), s32[]{:S(2)}) async-start(), calls=%async_computation.4 | async-start | bytes 1966080 | tf_op jit(solution)/shard_map/psum | solution.py:131
  11.9 5.6 %copy-start.6 = (bf16[192,128]{1,0:T(8,128)(2,1)S(1)}, bf16[192,128]{1,0:T(8,128)(2,1)}, u32[]{:S(2)}) copy-start(bf16[192,128]{1,0:T(8,128)(2,1)} %param.18) | copy-start | bytes 147460
  15.4 2.2 copy-start.3
  17.6 1.9 copy-start.2
  18.0 2.4 copy-start.4
  23.4 3.5 copy-start.5
  23.4 3.5 copy-start.12
  26.9 2.6 copy-start.7
  29.3 54.7 %copy-start.8 = (f32[2560]{0:T(1024)S(1)}, f32[2560]{0:T(1024)}, u32[]{:S(2)}) copy-start(f32[2560]{0:T(1024)} %param.27) | copy-start | bytes 30724
  29.3 395.0 %reduce-scatter.9.cloned.1.call-start = ((), (), s32[]{:S(2)}) async-start(), calls=%async_computation.6 | async-start | bytes 9830400
  236.9 9.0 %copy-start.9 = (bf16[2,384,2560]{2,1,0:T(8,128)(2,1)S(1)}, bf16[2,384,2560]{2,1,0:T(8,128)(2,1)}, u32[]{:S(2)}) copy-start(bf16[2,384,2560]{2,1,0:T(8,128)(2,1)} %param.31) | copy-start | bytes 11796484
  290.5 168.1 %reduce-scatter.7.cloned.1.call-start = ((), (), s32[]{:S(2)}) async-start(), calls=%async_computation.5 | async-start | bytes 1638400
  290.8 3.2 copy-start.10
  434.5 5.3 %copy-start.11 = (f32[2560,16]{0,1:T(8,128)S(1)}, f32[2560,16]{0,1:T(8,128)}, u32[]{:S(2)}) copy-start(f32[2560,16]{0,1:T(8,128)} %param.28) | copy-start | bytes 491524
  434.5 27.9 %all-to-all-start.1 = ((bf16[2,8,91,640]{3,0,2,1:T(2,128)(2,1)}), bf16[2,8,91,640]{3,0,2,1:T(2,128)(2,1)S(1)}, u32[]{:S(2)}, u32[]{:S(2)}) async-start(bf16[2,8,91,640]{3,0,2,1:T(2,128)(2,1)} %bitcast.151), calls=%async_computation.1 | async-start | bytes 3727360 | tf_op jit(solution)/shard_map/all_to_all | solution.py:152
  470.6 9.1 %copy-start.1 = (bf16[640,2560]{1,0:T(8,128)(2,1)S(1)}, bf16[640,2560]{1,0:T(8,128)(2,1)}, u32[]{:S(2)}) copy-start(bf16[640,2560]{1,0:T(8,128)(2,1)} %param.26) | copy-start | bytes 9830404
Sparse Core Ops, SparseCore 0:
  29.4 52.4 all-reduce.1
  290.6 133.7 reduce-scatter.8
  426.8 31.7 reduce-scatter.6
where the time goes:
time: 488 us; the launch traced here: 486 us
  waiting for transfers between devices  194 us (40%)
  local copies, waits for them, and re-layouts  140 us (29%)
  blocking collectives  87.5 us (18%)
  matrix products  31.1 us (6%)
  other arithmetic  16.7 us (3%)
  between operations  13.5 us (3%)
    unnamed x5, waiting for transfers between devices  144 us
    all_to_all x1, blocking collectives, shards(): lax.all_to_all(outbox, 'req', split_axis=1, concat_axis=1, tiled=True)  87.5 us
    unnamed x32, local copies, waits for them, and re-layouts  47.7 us
    psum x1, waiting for transfers between devices, shards(): lax.psum(attn_terms.astype(jnp.bfloat16), 'tp').astype(jnp.float32)  46.5 us
    reshape x2, local copies, waits for them, and re-layouts, fill_outbox(): return outbox.reshape(lead_shape + (row_values.shape[1],))  33.8 us
    scatter x1, local copies, waits for them, and re-layouts, fill_outbox(): outbox = outbox.at[slot_index].set(repeated)  17.2 us
    reshape x1, local copies, waits for them, and re-layouts, fill_outbox(): repeated = jnp.repeat(row_values, top_count, axis=0)  10.2 us
  transfers between devices with their start and end apart: 4, of which 4 were waited for; matrix products, arithmetic and copies ran while one was open for 5% of the time, Pallas kernels for 0%

commit v1 on v0

--- a/solution.py
+++ b/solution.py
@@ -128,7 +128,9 @@
     capacity = max(10 * requests, row_count * top_count * 5 // (4 * expert_count) + 1)
     slot_index = place_rows(routes, experts_local, groups, capacity)
     lead_shape = (experts_local, groups, capacity)
-    attn_out = lax.psum(attn_terms.astype(jnp.bfloat16), "tp").astype(jnp.float32)
+    attn_out = jnp.sum(lax.all_gather(attn_terms.astype(jnp.bfloat16), "tp"), axis=0).astype(
+        jnp.float32
+    )
     hidden = rounded(residual.astype(jnp.float32) + attn_out)
     rstd = lax.rsqrt(jnp.mean(hidden * hidden, axis=1, keepdims=True) + EPSILON)
     normed = hidden * rstd * norm_gain

time: 488 us -> 515 us (1.055)
  waiting for transfers between devices: 194 us -> 219 us
    all_gather x0 -> x1, waiting for transfers between devices: none -> 73.1 us  [shards(): lax.all_gather(attn_terms.astype(jnp.bfloat16), 'tp')]
    psum x1 -> x0, waiting for transfers between devices: 46.5 us -> none  [shards(): lax.psum(attn_terms.astype(jnp.bfloat16), 'tp').astype(jnp.float32)]
    unnamed x32 -> x34, local copies, waits for them, and re-layouts: 47.7 us -> 47.8 us
where the time goes in v1:
time: 515 us; the launch traced here: 514 us
  waiting for transfers between devices  219 us (43%)
  local copies, waits for them, and re-layouts  140 us (27%)
  blocking collectives  87.5 us (17%)
  matrix products  31.1 us (6%)
  other arithmetic  18.4 us (4%)
  between operations  13.5 us (3%)
    unnamed x5, waiting for transfers between devices  143 us
    all_to_all x1, blocking collectives, shards(): lax.all_to_all(outbox, 'req', split_axis=1, concat_axis=1, tiled=True)  87.5 us
    all_gather x1, waiting for transfers between devices, shards(): lax.all_gather(attn_terms.astype(jnp.bfloat16), 'tp')  73.1 us
    unnamed x34, local copies, waits for them, and re-layouts  47.8 us
    reshape x2, local copies, waits for them, and re-layouts, fill_outbox(): return outbox.reshape(lead_shape + (row_values.shape[1],))  33.8 us
    scatter x1, local copies, waits for them, and re-layouts, fill_outbox(): outbox = outbox.at[slot_index].set(repeated)  17.2 us
  transfers between devices with their start and end apart: 4, of which 4 were waited for; matrix products, arithmetic and copies ran while one was open for 5% of the time, Pallas kernels for 0%

profile of v1, /device:TPU:0, one launch (start us, length us, event | category | flops | bytes accessed | tf_op | source)
XLA Modules:
  0.0 513.8 jit_solution(17823615058921914805)
XLA Ops:
  6.6 0.8 compare_select_fusion.4
  7.5 0.8 iota_compare_fusion.5
  8.3 2.0 reshape.306
  10.2 1.0 convolution_minimum_fusion.5
  11.2 0.2 convolution_minimum_fusion.4
  11.5 0.2 convolution_minimum_fusion.3
  11.7 0.2 convolution_minimum_fusion.2
  11.9 0.2 convolution_minimum_fusion.1
  12.2 0.2 fusion.22
  12.4 0.1 copy.58
  12.5 2.9 gather_fusion.1
  15.4 2.1 bitcast_reduce_fusion
  17.6 0.4 fusion.55
  18.0 1.4 copy-done.2
  19.4 1.0 fusion.8
  20.4 0.1 fusion.28
  20.5 2.9 gather_fusion
  23.4 3.5 fusion.11
  26.9 0.3 fusion.21
  27.2 0.1 copy.61
  27.4 1.9 convolution_convert_fusion.2
  29.3 0.2 reduce-scatter.9.cloned.1.call-start
  29.5 0.1 copy.63
  29.7 0.1 eq.80
  29.8 0.1 eq.76
  29.9 0.1 reshape.311
  30.1 4.6 reduce-window.6
  34.7 0.4 slice_reduce_fusion
  35.1 0.2 reduce-window.9
  35.5 73.1 %all-gather.3.cloned.1.call-done = bf16[768,2560]{1,0:T(8,128)(2,1)} async-done(((bf16[192,2560]{1,0:T(8,128)(2,1)}), bf16[768,2560]{1,0:T(8,128)(2,1)}) %all-gather.3.cloned.1.call-update) | async-done | bytes 3932176 | tf_op jit(solution)/shard_map/all_gather | solution.py:131
  108.6 3.2 reduce_sum.79
  111.8 0.2 add_convert_fusion
  112.0 0.3 multiply_reduce_fusion.1
  112.3 0.3 fusion.15
  112.6 4.0 broadcast_in_dim.72
  116.6 10.2 %reshape.347 = bf16[1152,2560]{1,0:T(8,128)(2,1)} reshape(bf16[192,6,2560]{2,1,0:T(8,128)(2,1)} %broadcast_in_dim.72) | data formatting | bytes 11796480 | tf_op jit(solution)/shard_map/reshape | solution.py:72
  126.8 17.2 %scatter_custom_fusion = bf16[1456,2560]{1,0:T(8,128)(2,1)} fusion(s32[1152]{0:T(1024)S(1)} %fusion.48, bf16[1152,2560]{1,0:T(8,128)(2,1)} %reshape.347, bf16[]{:T(256)} %constant.69.clone.1), kind=kCustom, calls=%fused_computation.18 | custom fusion | bytes 7455232 | tf_op jit(solution)/shard_map/scatter | solution.py:76
  144.0 6.3 %reshape.314 = bf16[2,8,91,2560]{3,2,1,0:T(8,128)(2,1)} reshape(bf16[1456,2560]{1,0:T(8,128)(2,1)} %scatter_custom_fusion) | data formatting | bytes 14909440 | tf_op jit(solution)/shard_map/reshape | solution.py:77
  150.2 27.5 %copy.66 = bf16[2,8,91,2560]{3,0,2,1:T(2,128)(2,1)S(1)} copy(bf16[2,8,91,2560]{3,2,1,0:T(8,128)(2,1)} %reshape.314) | data formatting | bytes 14909440 | tf_op jit(solution)/shard_map/reshape | solution.py:77
  177.7 87.5 %all_to_all.10 = bf16[2,8,91,2560]{3,0,2,1:T(2,128)(2,1)S(1)} all-to-all(bf16[2,8,91,2560]{3,0,2,1:T(2,128)(2,1)S(1)} %copy.66), channel_id=1, replica_groups=mesh['req'=8,'tp'=4] {'req'}, dimensions={1} | all-to-all | bytes 14909440 | tf_op jit(solution)/shard_map/all_to_all | solution.py:141
  265.2 9.0 %fusion = f32[2,728,2,384]{3,1,2,0:T(8,128)S(1)} fusion(bf16[2,2560,2,384]{3,2,1,0:T(2,128)(2,1)} %param.30, bf16[2,728,2560,1]{2,0,1,3:T(2,128)(2,1)S(1)} %bitcast.151), kind=kOutput, calls=%fused_computation.4 | convolution fusion | flops 5725224960 | bytes 19791872 | tf_op jit(solution)/shard_map/emd,edcf->emcf/dot_general | solution.py:143
  274.3 6.2 %convolution_convert_fusion = bf16[2,728,2560]{2,1,0:T(8,128)(2,1)} fusion(bf16[2,384,2560]{2,1,0:T(8,128)(2,1)S(1)} %copy-done.10, f32[2,728,2,384]{3,1,2,0:T(8,128)S(1)} %fusion), kind=kOutput, calls=%fused_computation.7 | convolution fusion | flops 2869694464 | bytes 15859712 | tf_op jit(solution)/shard_map/emf,efd->emd/dot_general | solution.py:148
  280.4 20.1 %copy.85 = bf16[2,728,2560]{1,0,2:T(2,128)(2,1)} copy(bf16[2,728,2560]{2,1,0:T(8,128)(2,1)} %convolution_convert_fusion) | data formatting | bytes 14909440
  300.5 18.3 %reshape.366 = bf16[2560,1456]{1,0:T(8,128)(2,1)} reshape(bf16[2560,2,728]{2,1,0:T(2,128)(2,1)} %bitcast.149) | data formatting | bytes 14909440
  318.8 0.3 reduce-scatter.7.cloned.1.call-start
  319.2 3.2 fusion.4
  322.4 0.7 convolution_convert_fusion.1
  323.1 1.4 copy.83
  324.5 127.4 %reduce-scatter.9.cloned.1.call-done = bf16[640,1456]{1,0:T(8,128)(2,1)} async-done(((bf16[2560,1456]{1,0:T(8,128)(2,1)}), bf16[640,1456]{1,0:T(8,128)(2,1)}) %reduce-scatter.9.cloned.1.call-update) | async-done | bytes 1863696
  451.9 5.2 %reshape.367 = bf16[640,2,728]{2,1,0:T(2,128)(2,1)S(1)} reshape(bf16[640,1456]{1,0:T(8,128)(2,1)} %reduce-scatter.9.cloned.1.call-done) | data formatting | bytes 3727360
  457.1 5.0 copy.82
  462.1 3.8 all-to-all-start.1
  465.9 1.5 convert_element_type.79
  467.4 1.8 fusion.14
  469.2 0.8 copy.72
  470.0 16.0 %reduce-scatter.7.cloned.1.call-done = bf16[640,192]{1,0:T(8,128)(2,1)} async-done(((bf16[2560,192]{1,0:T(8,128)(2,1)}), bf16[640,192]{1,0:T(8,128)(2,1)}) %reduce-scatter.7.cloned.1.call-update) | async-done | bytes 245776
  486.0 1.1 copy.84
  487.2 2.8 all-to-all-done.1
  490.0 1.5 copy.71
  491.5 1.8 reshape.317
  493.3 4.8 gather_fusion.2
  498.1 4.0 reshape.318
  502.1 3.4 multiply_reduce_fusion
  505.5 1.8 add_convert_fusion.1
  (45 shorter events, 0.5 us)
Async XLA Ops:
  6.5 20.8 %copy-start = (bf16[640,2560]{1,0:T(8,128)(2,1)S(1)}, bf16[640,2560]{1,0:T(8,128)(2,1)}, u32[]{:S(2)}) copy-start(bf16[640,2560]{1,0:T(8,128)(2,1)} %param.26) | copy-start | bytes 9830404
  6.5 102.0 %all-gather.3.cloned.1.call-start = ((), (), s32[]{:S(2)}) async-start(), calls=%async_computation.4 | async-start | bytes 4915200 | tf_op jit(solution)/shard_map/all_gather | solution.py:131
  11.9 5.6 %copy-start.7 = (bf16[192,128]{1,0:T(8,128)(2,1)S(1)}, bf16[192,128]{1,0:T(8,128)(2,1)}, u32[]{:S(2)}) copy-start(bf16[192,128]{1,0:T(8,128)(2,1)} %param.18) | copy-start | bytes 147460
  15.4 2.2 copy-start.3
  17.6 1.9 copy-start.2
  18.0 2.4 copy-start.4
  23.4 3.5 copy-start.5
  23.4 3.5 copy-start.13
  26.9 2.6 copy-start.8
  29.3 82.5 %copy-start.6 = (bf16[192,2560]{1,0:T(8,128)(2,1)S(1)}, bf16[192,2560]{1,0:T(8,128)(2,1)}, u32[]{:S(2)}) copy-start(bf16[192,2560]{1,0:T(8,128)(2,1)} %param.25) | copy-start | bytes 2949124
  29.3 422.6 %reduce-scatter.9.cloned.1.call-start = ((), (), s32[]{:S(2)}) async-start(), calls=%async_computation.6 | async-start | bytes 9830400
  108.6 3.7 copy-start.9
  265.2 9.0 %copy-start.10 = (bf16[2,384,2560]{2,1,0:T(8,128)(2,1)S(1)}, bf16[2,384,2560]{2,1,0:T(8,128)(2,1)}, u32[]{:S(2)}) copy-start(bf16[2,384,2560]{2,1,0:T(8,128)(2,1)} %param.31) | copy-start | bytes 11796484
  318.8 167.2 %reduce-scatter.7.cloned.1.call-start = ((), (), s32[]{:S(2)}) async-start(), calls=%async_computation.5 | async-start | bytes 1638400
  319.1 3.2 copy-start.11
  462.1 5.3 %copy-start.12 = (f32[2560,16]{0,1:T(8,128)S(1)}, f32[2560,16]{0,1:T(8,128)}, u32[]{:S(2)}) copy-start(f32[2560,16]{0,1:T(8,128)} %param.28) | copy-start | bytes 491524
  462.1 27.9 %all-to-all-start.1 = ((bf16[2,8,91,640]{3,0,2,1:T(2,128)(2,1)}), bf16[2,8,91,640]{3,0,2,1:T(2,128)(2,1)S(1)}, u32[]{:S(2)}, u32[]{:S(2)}) async-start(bf16[2,8,91,640]{3,0,2,1:T(2,128)(2,1)} %bitcast.152), calls=%async_computation.1 | async-start | bytes 3727360 | tf_op jit(solution)/shard_map/all_to_all | solution.py:154
  498.1 9.1 %copy-start.1 = (bf16[640,2560]{1,0:T(8,128)(2,1)S(1)}, bf16[640,2560]{1,0:T(8,128)(2,1)}, u32[]{:S(2)}) copy-start(bf16[640,2560]{1,0:T(8,128)(2,1)} %param.26) | copy-start | bytes 9830404
Sparse Core Ops, SparseCore 0:
  29.4 79.1 all-gather.2
  319.0 132.9 reduce-scatter.8
  454.2 31.7 reduce-scatter.6
